TPU v7x, 256 devices: a whole 4x4x8 slice. The times are simulated.
256 devices in a mesh: dp: 2 (over y_hi), retr: 16 (over x, y_lo, core), tensor: 8 (over z).
Axes of the slice: x: 4, y: 4 (y_hi: 2, y_lo: 2; y = y_hi * 2 + y_lo), z: 8, core: 2. Of those that a mesh axis runs over, the one named last changes fastest.
Arguments:
- hidden_in: bfloat16 [16384, 4096], P(('dp', 'retr'), 'tensor'), may hold values from -12 to 12
- norm_gain: float32 [4096], replicated, may hold values from 0.1 to 1.9
- nbr_table: int32 [256, 2], P(('dp', 'retr')), may hold values from 0 to 63, as said below
- encodings: bfloat16 [64, 128, 1024], P('retr'), may hold values from -21 to 21
- enc_mask: int32 [64, 4], P('retr'), may hold values from 0 to 1, as said below
- w_query: bfloat16 [4096, 4096], P(None, 'tensor'), may hold values from -0.02703125 to 0.02703125
- w_key: bfloat16 [1024, 4096], P(None, 'tensor'), may hold values from -0.1021875 to 0.1021875
- w_value: bfloat16 [1024, 4096], P(None, 'tensor'), may hold values from -0.1875 to 0.1875
- w_out: bfloat16 [4096, 4096], P('tensor'), may hold values from -0.125 to 0.125
Outputs:
- mixed: bfloat16 [16384, 4096], P(('dp', 'retr'), 'tensor')
Inputs may be any that keep to these rules, and one draw needn't show every extreme that they name: `nbr_table`: each aligned block of 8 table rows (the rows of one device) holds 16 distinct ids; at most 2 of them share the value id // 4, and in every block some value of id // 4 has exactly 2. `enc_mask`: in each row the ones come first; the first entry is 1.
All inputs are finite; a program needn't handle non-finite values.
Results may differ from a plain program's by a relative error of at most 0.012.
The roundings to bfloat16 on the way count: a program that leaves them out, or rounds other values in their place, can miss the bound.
Values may be sent and summed in bfloat16 or wider, within the bound.
No kernel may reach another device: no remote copies, remote signals or barrier semaphores. Data moves between devices by JAX's collectives and lax.ppermute only.
A program may use at most 128 MiB of HBM per device.

v0:
```python
import math
import jax
import jax.numpy as jnp
from jax import lax
from jax.sharding import PartitionSpec as P

HD = 128
NBRS = 2
BLOCK = 32


def attend_gathered(queries, key_value, selected_marks, segment_count, head_cols):
    tok_rows = queries.shape[0]
    head_count = head_cols // HD
    entry_keys = key_value.shape[0] // segment_count * key_value.shape[1]
    mask_cols = selected_marks.shape[1]
    key_block = key_value[:, :, :head_cols].reshape(segment_count, entry_keys, head_count, HD)
    value_block = key_value[:, :, head_cols:].reshape(segment_count, entry_keys, head_count, HD)
    key_live = (
        jnp.repeat(selected_marks.reshape(segment_count, NBRS * mask_cols), BLOCK, axis=1) > 0
    )
    query_block = queries.reshape(segment_count, tok_rows // segment_count, head_count, HD)
    factor = 1.0 / math.sqrt(HD)
    scores = (
        jnp.einsum("cqhd,ckhd->chqk", query_block, key_block, preferred_element_type=jnp.float32)
        * factor
    )
    key_open = key_live[:, None, None, :]
    scores = jnp.where(key_open, scores, -1e30)
    row_max = jnp.max(scores, axis=-1, keepdims=True)
    weights = jnp.exp(scores - row_max) * key_open.astype(jnp.float32)
    probabilities = (weights / jnp.sum(weights, axis=-1, keepdims=True)).astype(jnp.bfloat16)
    attended = jnp.einsum(
        "chqk,ckhd->cqhd", probabilities, value_block, preferred_element_type=jnp.float32
    )
    return attended.astype(jnp.bfloat16).reshape(tok_rows, head_cols)


def local(hidden_in, norm_gain, nbr_table, encodings, enc_mask, w_query, w_key, w_value, w_out):
    gathered = lax.all_gather(hidden_in, "tensor", axis=1, tiled=True)
    widened = gathered.astype(jnp.float32)
    mean_sq = jnp.mean(widened * widened, axis=-1, keepdims=True)
    normed = (widened * lax.rsqrt(mean_sq + 1e-05) * norm_gain).astype(jnp.bfloat16)
    queries = jnp.dot(normed, w_query, preferred_element_type=jnp.float32).astype(jnp.bfloat16)
    w_both = jnp.concatenate([w_key, w_value], axis=1)
    segment_count = nbr_table.shape[0]
    entry_len = encodings.shape[1]
    enc_width = encodings.shape[2]
    head_cols = w_key.shape[1]
    wanted = nbr_table.reshape(-1)
    need_count = wanted.shape[0]
    live_marks = enc_mask.astype(jnp.bfloat16)
    entry_rows = lax.all_gather(encodings, "retr", axis=0, tiled=True)
    entry_marks = lax.all_gather(live_marks, "retr", axis=0, tiled=True)
    piece_count = entry_rows.shape[0]
    one_hot = (wanted[:, None] == jnp.arange(piece_count, dtype=jnp.int32)[None, :]).astype(
        jnp.bfloat16
    )
    picked = jnp.einsum(
        "jn,nre->jre", one_hot, entry_rows, preferred_element_type=jnp.float32
    ).astype(jnp.bfloat16)
    picked_marks = jnp.dot(one_hot, entry_marks, preferred_element_type=jnp.float32).astype(
        jnp.bfloat16
    )
    key_value = jnp.dot(
        picked.reshape(need_count * entry_len, enc_width),
        w_both,
        preferred_element_type=jnp.float32,
    )
    key_value = key_value.astype(jnp.bfloat16).reshape(need_count, entry_len, 2 * head_cols)
    attended = attend_gathered(queries, key_value, picked_marks, segment_count, head_cols)
    partial_value = jnp.dot(attended, w_out, preferred_element_type=jnp.float32)
    summed = lax.psum_scatter(partial_value, "tensor", scatter_dimension=1, tiled=True)
    return (hidden_in.astype(jnp.float32) + summed).astype(jnp.bfloat16)


def solution(mesh):
    in_specs = (
        P(("dp", "retr"), "tensor"),
        P(),
        P(("dp", "retr"), None),
        P("retr", None, None),
        P("retr", None),
        P(None, "tensor"),
        P(None, "tensor"),
        P(None, "tensor"),
        P("tensor", None),
    )
    out_specs = P(("dp", "retr"), "tensor")
    return jax.shard_map(local, mesh=mesh, in_specs=in_specs, out_specs=out_specs, check_vma=False)
```

profile of v0, /device:TPU:1, one launch (start us, length us, event | category | flops | bytes accessed | tf_op | source)
XLA Modules:
  0.0 318.5 jit_solution(9526612523659051779)
XLA Ops:
  6.5 0.0 copy-start.6
  6.5 0.0 all-gather.6.cloned.1.call-start
  6.5 0.7 all-gather.6.cloned.1.call-update
  7.3 0.0 all-gather.4.cloned.1.call-start
  7.3 0.7 all-gather.4.cloned.1.call-update
  8.0 0.0 reduce-scatter.2.cloned.1.call-start
  8.1 0.8 copy.24
  8.8 0.1 eq.15
  8.9 0.7 convert_bitcast_fusion
  9.6 21.0 %all-gather = bf16[16,4,4]{2,1,0:T(4,128)(2,1)S(1)} all-gather(bf16[1,4,4]{2,1,0:T(4,128)(2,1)S(1)} %convert_bitcast_fusion), channel_id=1, replica_groups=mesh['dp'=2,'retr'=16,'tensor'=8] {'retr'}, dimensions={0}, use_global_device_ids=true | all-gather | bytes 544 | tf_op jit(solution)/shard_map/all_gather | solution.py:54
  30.6 0.2 fusion.30
  30.8 0.1 copy.28
  30.9 0.1 gt.22
  31.0 0.1 broadcast_in_dim.14
  31.0 0.1 gt.23
  31.2 36.4 %all-gather.6.cloned.1.call-done = bf16[512,4096]{1,0:T(8,128)(2,1)} async-done(((bf16[512,512]{1,0:T(8,128)(2,1)}), bf16[512,4096]{1,0:T(8,128)(2,1)}) %all-gather.6.cloned.1.call-update) | async-done | bytes 4194320 | tf_op jit(solution)/shard_map/all_gather | solution.py:40
  67.5 0.0 copy-start.1
  67.5 3.2 %fusion.3 = f32[512]{0:T(512)S(1)} fusion(bf16[512,4096]{1,0:T(8,128)(2,1)} %all-gather.6.cloned.1.call-done), kind=kLoop, calls=%fused_computation.5 | loop fusion | flops 6290944 | bytes 4196352 | tf_op jit(solution)/shard_map/reduce_sum | solution.py:42
  70.8 0.0 copy-done.6
  70.8 0.2 copy-done.1
  71.0 4.6 %fusion.24 = bf16[512,512]{1,0:T(8,128)(2,1)S(1)} fusion(bf16[4096,512]{1,0:T(8,128)(2,1)} %param.14, bf16[512,4096]{1,0:T(8,128)(2,1)S(1)} %copy-done.1, f32[4096]{0:T(1024)S(1)} %copy-done.6, f32[512]{0:T(512)S(1)} %add_rsqrt_fusion), kind=kOutput, calls=%fused_computation.25 | convolution fusion | flops 2156134400 | bytes 8931328 | tf_op jit(solution)/shard_map/dot_general | solution.py:44
  75.6 0.1 reshape.49
  75.7 87.0 %all-gather.4.cloned.1.call-done = bf16[64,128,1024]{2,1,0:T(8,128)(2,1)} async-done(((bf16[4,128,1024]{2,1,0:T(8,128)(2,1)}), bf16[64,128,1024]{2,1,0:T(8,128)(2,1)}) %all-gather.4.cloned.1.call-update) | async-done | bytes 16777232 | tf_op jit(solution)/shard_map/all_gather | solution.py:53
  162.7 23.7 %fusion.10 = bf16[16,128,1024]{2,0,1:T(8,128)(2,1)S(1)} fusion(bf16[64,128,1024]{2,1,0:T(8,128)(2,1)} %all-gather.4.cloned.1.call-done, s32[16]{0:T(128)S(1)} %eq.15), kind=kOutput, calls=%fused_computation.12 | convolution fusion | flops 270533632 | bytes 20971584 | tf_op jit(solution)/shard_map/jn,nre->jre/dot_general | solution.py:59
  186.4 0.0 copy-start.4
  186.4 0.0 copy-start.5
  186.4 2.5 copy.26
  188.9 0.0 copy-done.4
  189.0 0.0 copy-done.5
  189.0 5.0 %convolution_convert_fusion = bf16[2048,1024]{1,0:T(8,128)(2,1)S(1)} fusion(bf16[2048,1024]{1,0:T(8,128)(2,1)S(1)} %bitcast.20, bf16[1024,512]{1,0:T(8,128)(2,1)S(1)} %copy-done.4, bf16[1024,512]{1,0:T(8,128)(2,1)S(1)} %copy-done.5), kind=kOutput, calls=%fused_computation.11 | convolution fusion | flops 4301258752 | bytes 10485760 | tf_op jit(solution)/shard_map/dot_general | solution.py:65
  194.0 1.8 fusion.46
  195.8 4.0 %reshape.55 = bf16[8,256,4,128]{3,2,1,0:T(4,128)(2,1)} reshape(bf16[16,128,512]{2,1,0:T(8,128)(2,1)} %get-tuple-element.5) | data formatting | bytes 4194304 | tf_op jit(solution)/shard_map/reshape | solution.py:17
  199.8 2.0 reshape.56
  201.8 0.0 copy-start.2
  201.8 4.1 %fusion.47 = (f32[8,4,64]{2,1,0:T(4,128)S(1)}, f32[8,4,64,256]{3,2,1,0:T(8,128)}) fusion(f32[8,256]{1,0:T(8,128)S(1)} %convert_element_type.53, pred[8,256]{1,0:T(8,128)(4,1)S(1)} %gt.23, bf16[8,256,4,128]{3,2,1,0:T(4,128)(2,1)} %reshape.55, bf16[8,64,4,128]{3,2,1,0:T(4,128)(2,1)S(1)} %reshape.49), kind=kOutput, calls=%fused_computation.48 | convolution fusion | flops 136839424 | bytes 4737024 | tf_op jit(solution)/shard_map/sub | solution.py:31
  206.0 0.0 copy-done.2
  206.0 0.0 copy-start
  206.0 2.3 fusion.27
  208.3 0.4 copy.33
  208.7 0.1 copy-done
  208.8 5.6 %fusion.35 = f32[512,4096]{1,0:T(8,128)} fusion(bf16[512,4096]{1,0:T(8,128)(2,1)S(1)} %copy-done, bf16[64,8,4,128]{3,2,1,0:T(4,128)(2,1)S(1)} %bitcast.21), kind=kOutput, calls=%fused_computation.34 | convolution fusion | flops 2147483648 | bytes 13107200 | tf_op jit(solution)/shard_map/dot_general | solution.py:72
  214.4 0.0 copy-start.3
  214.4 0.0 reduce-scatter.2.cloned.1.call-update
  214.4 95.4 %reduce-scatter.2.cloned.1.call-done = f32[512,512]{1,0:T(8,128)} async-done(((f32[512,4096]{1,0:T(8,128)}), f32[512,512]{1,0:T(8,128)}) %reduce-scatter.2.cloned.1.call-update) | async-done | bytes 1048592 | tf_op jit(solution)/shard_map/reduce_scatter | solution.py:73
  309.8 0.0 copy-done.3
  309.8 2.2 add_convert_fusion
  (2 shorter events, 0.0 us)
Async XLA Ops:
  6.5 64.2 %copy-start.6 = (f32[4096]{0:T(1024)S(1)}, f32[4096]{0:T(1024)}, u32[]{:S(2)}) copy-start(f32[4096]{0:T(1024)} %param.10) | copy-start | bytes 49156
  6.5 61.0 %all-gather.6.cloned.1.call-start = ((), (), s32[]{:S(2)}) async-start(), calls=%async_computation.2 | async-start | bytes 4718592 | tf_op jit(solution)/shard_map/all_gather | solution.py:40
  7.3 155.4 %all-gather.4.cloned.1.call-start = ((), (), s32[]{:S(2)}) async-start(), calls=%async_computation.1 | async-start | bytes 17825792 | tf_op jit(solution)/shard_map/all_gather | solution.py:53
  8.0 301.8 %reduce-scatter.2.cloned.1.call-start = ((), (), s32[]{:S(2)}) async-start(), calls=%async_computation.3 | async-start | bytes 9437184 | tf_op jit(solution)/shard_map/reduce_scatter | solution.py:73
  67.5 3.4 %copy-start.1 = (bf16[512,4096]{1,0:T(8,128)(2,1)S(1)}, bf16[512,4096]{1,0:T(8,128)(2,1)}, u32[]{:S(2)}) copy-start(bf16[512,4096]{1,0:T(8,128)(2,1)} %all-gather.6.cloned.1.call-done) | copy-start | bytes 12582916
  186.4 2.6 copy-start.4
  186.4 2.6 copy-start.5
  201.8 4.2 %copy-start.2 = (bf16[8,256,4,128]{3,2,1,0:T(4,128)(2,1)S(1)}, bf16[8,256,4,128]{3,2,1,0:T(4,128)(2,1)}, u32[]{:S(2)}) copy-start(bf16[8,256,4,128]{3,2,1,0:T(4,128)(2,1)} %reshape.56) | copy-start | bytes 6291460
  206.0 2.8 copy-start
  214.4 95.4 %copy-start.3 = (bf16[512,512]{1,0:T(8,128)(2,1)S(1)}, bf16[512,512]{1,0:T(8,128)(2,1)}, u32[]{:S(2)}) copy-start(bf16[512,512]{1,0:T(8,128)(2,1)} %param.9) | copy-start | bytes 1572868
Sparse Core Ops, SparseCore 0:
  9.1 58.3 all-gather.5
  69.4 93.2 all-gather.3
  214.5 95.2 reduce-scatter.1
where the time goes:
time: 319 us
  waiting for transfers between devices  220 us (69%)
  matrix products  45.5 us (14%)
  blocking collectives  21 us (7%)
  between operations  13.2 us (4%)
  local copies, waits for them, and re-layouts  12.5 us (4%)
  other arithmetic  6.11 us (2%)
    reduce_scatter x1, waiting for transfers between devices, local(): lax.psum_scatter(partial_value, 'tensor', scatter_dimension=1, tiled=True)  95.4 us
    all_gather x1, waiting for transfers between devices, local(): entry_rows = lax.all_gather(encodings, 'retr', axis=0, tiled=True)  87 us
    all_gather x1, waiting for transfers between devices, local(): gathered = lax.all_gather(hidden_in, 'tensor', axis=1, tiled=True)  36.4 us
    dot_general x1, matrix products, local(): jnp.einsum('jn,nre->jre', one_hot, entry_rows, preferred_element_type=jnp...  23.7 us
    all_gather x1, blocking collectives, local(): entry_marks = lax.all_gather(live_marks, 'retr', axis=0, tiled=True)  21 us
  transfers between devices with their start and end apart: 3, of which 3 were waited for; matrix products, arithmetic and copies ran while one was open for 3% of the time, Pallas kernels for 0%

commit v1 on v0

--- a/solution.py
+++ b/solution.py
@@ -37,7 +37,45 @@
 
 
 def local(hidden_in, norm_gain, nbr_table, encodings, enc_mask, w_query, w_key, w_value, w_out):
-    gathered = lax.all_gather(hidden_in, "tensor", axis=1, tiled=True)
+
+    def _bring_group(mat, dim_k):
+        z1, current_arr, q_next = (
+            lax.axis_size("tensor"),
+            lax.axis_index("tensor"),
+            mat.shape[dim_k],
+        )
+        panels = []
+        for c, num in enumerate(mat.shape):
+            panels.append(num * z1 if c == dim_k else num)
+        near = lax.dynamic_update_slice_in_dim(
+            jnp.zeros(panels, mat.dtype), mat, current_arr * q_next, axis=dim_k
+        )
+        high = tmp = mat
+        pp = 1
+        while pp < z1 // 2 + 1:
+            buffer = []
+            c = 0
+            while c < z1:
+                buffer.append((c, (c + 1) % z1))
+                c += 1
+            high = lax.ppermute(high, "tensor", buffer)
+            near = lax.dynamic_update_slice_in_dim(
+                near, high, (current_arr - pp) % z1 * q_next, axis=dim_k
+            )
+            if 2 * pp < z1:
+                items = []
+                c = 0
+                while c < z1:
+                    items.append((c, (c - 1) % z1))
+                    c = c + 1
+                tmp = lax.ppermute(tmp, "tensor", perm=items)
+                near = lax.dynamic_update_slice_in_dim(
+                    near, tmp, (current_arr + pp) % z1 * q_next, axis=dim_k
+                )
+            pp = pp + 1
+        return near
+
+    gathered = _bring_group(hidden_in, 1)
     widened = gathered.astype(jnp.float32)
     mean_sq = jnp.mean(widened * widened, axis=-1, keepdims=True)
     normed = (widened * lax.rsqrt(mean_sq + 1e-05) * norm_gain).astype(jnp.bfloat16)

time: 319 us -> 269 us (0.84); the launches traced: 319 us -> 264 us
  waiting for transfers between devices: 220 us -> 155 us
  starting transfers between devices: 0.08 us -> 12.9 us
    all_gather x1, waiting for transfers between devices: 87 us -> 22.8 us  [local(): entry_rows = lax.all_gather(encodings, 'retr', axis=0, tiled=True)]
    all_gather x1 -> x0, waiting for transfers between devices: 36.4 us -> none  [local(): gathered = lax.all_gather(hidden_in, 'tensor', axis=1, tiled=True)]
    ppermute x0 -> x7, waiting for transfers between devices: none -> 36.4 us  [the longest x4 26.2 us: _bring_group(): high = lax.ppermute(high, 'tensor', buffer)]
    ppermute x0 -> x7, starting transfers between devices: none -> 12.8 us  [the longest x3 9.73 us: _bring_group(): tmp = lax.ppermute(tmp, 'tensor', perm=items)]
  transfers between devices with their start and end apart: 3 -> 9, of which waited for: 3 -> 6; matrix products, arithmetic and copies ran while one was open for 3% -> 2% of each run, Pallas kernels for 0% -> 0%
where the time goes in v1:
time: 269 us; the launch traced here: 264 us
  waiting for transfers between devices  155 us (58%)
  matrix products  43.4 us (16%)
  blocking collectives  21.6 us (8%)
  between operations  13.9 us (5%)
  local copies, waits for them, and re-layouts  13.3 us (5%)
  starting transfers between devices  12.9 us (5%)
  other arithmetic  3.77 us (1%)
    reduce_scatter x1, waiting for transfers between devices, local(): lax.psum_scatter(partial_value, 'tensor', scatter_dimension=1, tiled=True)  95.3 us
    ppermute x4, waiting for transfers between devices, _bring_group(): high = lax.ppermute(high, 'tensor', buffer)  26.2 us
    dot_general x1, matrix products, local(): jnp.einsum('jn,nre->jre', one_hot, entry_rows, preferred_element_type=jnp...  23.7 us
    all_gather x1, waiting for transfers between devices, local(): entry_rows = lax.all_gather(encodings, 'retr', axis=0, tiled=True)  22.8 us
    all_gather x1, blocking collectives, local(): entry_marks = lax.all_gather(live_marks, 'retr', axis=0, tiled=True)  21.6 us
    ppermute x3, waiting for transfers between devices, _bring_group(): tmp = lax.ppermute(tmp, 'tensor', perm=items)  10.2 us
    ppermute x3, starting transfers between devices, _bring_group(): tmp = lax.ppermute(tmp, 'tensor', perm=items)  9.73 us
    dot_general x1, matrix products, local(): partial_value = jnp.dot(attended, w_out, preferred_element_type=jnp.float32)  5.58 us
  transfers between devices with their start and end apart: 9, of which 6 were waited for; matrix products, arithmetic and copies ran while one was open for 2% of the time, Pallas kernels for 0%

profile of v1, /device:TPU:1, one launch (start us, length us, event | category | flops | bytes accessed | tf_op | source)
XLA Modules:
  0.0 264.0 jit_solution(16003584664022747254)
XLA Ops:
  6.5 0.7 all-gather.3.cloned.1.call-update
  7.3 0.0 reduce-scatter.2.cloned.1.call-start
  7.3 2.5 collective-permute-start
  9.8 4.0 %collective-permute-start.1 = (bf16[512,512]{1,0:T(8,128)(2,1)}, bf16[512,512]{1,0:T(8,128)(2,1)S(1)}, u32[]{:S(2)}, u32[]{:S(2)}) collective-permute-start(bf16[512,512]{1,0:T(8,128)(2,1)} %param.9), channel_id=1, source_target_pairs={{0,7},{1,0},{2,1},{3,2},{4,3},{5,4},{6,5},{7,6},{8,15},{9,8},{10,9... | collective-permute-start | bytes 1572872 | tf_op jit(solution)/shard_map/ppermute | solution.py:71
  13.9 11.7 %collective-permute-done = bf16[512,512]{1,0:T(8,128)(2,1)S(1)} collective-permute-done((bf16[512,512]{1,0:T(8,128)(2,1)}, bf16[512,512]{1,0:T(8,128)(2,1)S(1)}, u32[]{:S(2)}, u32[]{:S(2)}) %collective-permute-start) | collective-permute-done | bytes 524320 | tf_op jit(solution)/shard_map/ppermute | solution.py:61
  25.6 2.7 %collective-permute-start.3 = (bf16[512,512]{1,0:T(8,128)(2,1)S(1)}, bf16[512,512]{1,0:T(8,128)(2,1)S(1)}, u32[]{:S(2)}, u32[]{:S(2)}) collective-permute-start(bf16[512,512]{1,0:T(8,128)(2,1)S(1)} %collective-permute-done.1), channel_id=1, source_target_pairs={{0,7},{1,0},{2,1},{3,2},{4,3},{5,4},{6,5},{7,6},{8,15},{9,8},{10,9... | collective-permute-start | bytes 1572872 | tf_op jit(solution)/shard_map/ppermute | solution.py:71
  28.3 10.8 %collective-permute-done.2 = bf16[512,512]{1,0:T(8,128)(2,1)S(1)} collective-permute-done((bf16[512,512]{1,0:T(8,128)(2,1)S(1)}, bf16[512,512]{1,0:T(8,128)(2,1)S(1)}, u32[]{:S(2)}, u32[]{:S(2)}) %collective-permute-start.2) | collective-permute-done | bytes 524320 | tf_op jit(solution)/shard_map/ppermute | solution.py:61
  39.1 0.7 convert_bitcast_fusion
  39.7 0.8 copy.24
  40.5 0.1 eq.23
  40.6 21.6 %all-gather = bf16[16,4,4]{2,1,0:T(4,128)(2,1)S(1)} all-gather(bf16[1,4,4]{2,1,0:T(4,128)(2,1)S(1)} %convert_bitcast_fusion), channel_id=1, replica_groups=mesh['dp'=2,'retr'=16,'tensor'=8] {'retr'}, dimensions={0}, use_global_device_ids=true | all-gather | bytes 544 | tf_op jit(solution)/shard_map/all_gather | solution.py:92
  62.2 0.2 fusion.30
  62.4 0.1 copy.28
  62.5 0.1 gt.22
  62.6 0.1 broadcast_in_dim.24
  62.7 0.1 gt.23
  62.8 0.5 broadcast_in_dim.26
  63.3 0.1 constant_dynamic-update-slice_fusion.7
  63.4 3.0 %collective-permute-start.5 = (bf16[512,512]{1,0:T(8,128)(2,1)S(1)}, bf16[512,512]{1,0:T(8,128)(2,1)S(1)}, u32[]{:S(2)}, u32[]{:S(2)}) collective-permute-start(bf16[512,512]{1,0:T(8,128)(2,1)S(1)} %collective-permute-done.3), channel_id=1, source_target_pairs={{0,7},{1,0},{2,1},{3,2},{4,3},{5,4},{6,5},{7,6},{8,15},{9,8},{10,9... | collective-permute-start | bytes 1572872 | tf_op jit(solution)/shard_map/ppermute | solution.py:71
  66.4 0.1 constant_dynamic-update-slice_fusion.6
  66.5 0.5 collective-permute-start.6
  67.1 0.1 constant_dynamic-update-slice_fusion.5
  67.1 0.1 constant_dynamic-update-slice_fusion.4
  67.2 0.0 copy-start.3
  67.3 0.1 constant_dynamic-update-slice_fusion.3
  67.3 0.1 constant_dynamic-update-slice_fusion.2
  67.4 10.1 %collective-permute-done.5 = bf16[512,512]{1,0:T(8,128)(2,1)S(1)} collective-permute-done((bf16[512,512]{1,0:T(8,128)(2,1)S(1)}, bf16[512,512]{1,0:T(8,128)(2,1)S(1)}, u32[]{:S(2)}, u32[]{:S(2)}) %collective-permute-start.5) | collective-permute-done | bytes 524320 | tf_op jit(solution)/shard_map/ppermute | solution.py:71
  77.6 0.1 constant_dynamic-update-slice_fusion.1
  77.6 3.7 %collective-permute-done.6 = bf16[512,512]{1,0:T(8,128)(2,1)S(1)} collective-permute-done((bf16[512,512]{1,0:T(8,128)(2,1)S(1)}, bf16[512,512]{1,0:T(8,128)(2,1)S(1)}, u32[]{:S(2)}, u32[]{:S(2)}) %collective-permute-start.6) | collective-permute-done | bytes 524320 | tf_op jit(solution)/shard_map/ppermute | solution.py:61
  81.3 0.1 constant_dynamic-update-slice_fusion
  81.4 0.9 fusion.3
  82.3 2.5 fusion.24
  84.8 0.1 reshape.49
  84.9 22.8 %all-gather.3.cloned.1.call-done = bf16[64,128,1024]{2,1,0:T(8,128)(2,1)} async-done(((bf16[4,128,1024]{2,1,0:T(8,128)(2,1)}), bf16[64,128,1024]{2,1,0:T(8,128)(2,1)}) %all-gather.3.cloned.1.call-update) | async-done | bytes 16777232 | tf_op jit(solution)/shard_map/all_gather | solution.py:91
  107.7 23.7 %fusion.10 = bf16[16,128,1024]{2,0,1:T(8,128)(2,1)S(1)} fusion(bf16[64,128,1024]{2,1,0:T(8,128)(2,1)} %all-gather.3.cloned.1.call-done, s32[16]{0:T(128)S(1)} %eq.23), kind=kOutput, calls=%fused_computation.12 | convolution fusion | flops 270533632 | bytes 20971584 | tf_op jit(solution)/shard_map/jn,nre->jre/dot_general | solution.py:97
  131.4 2.5 copy.26
  133.9 5.0 %convolution_convert_fusion = bf16[2048,1024]{1,0:T(8,128)(2,1)S(1)} fusion(bf16[2048,1024]{1,0:T(8,128)(2,1)S(1)} %bitcast.20, bf16[1024,512]{1,0:T(8,128)(2,1)S(1)} %copy-done.4, bf16[1024,512]{1,0:T(8,128)(2,1)S(1)} %copy-done.5), kind=kOutput, calls=%fused_computation.11 | convolution fusion | flops 4301258752 | bytes 10485760 | tf_op jit(solution)/shard_map/dot_general | solution.py:103
  138.9 1.8 fusion.46
  140.8 4.0 %reshape.56 = bf16[8,256,4,128]{3,2,1,0:T(4,128)(2,1)} reshape(bf16[16,128,512]{2,1,0:T(8,128)(2,1)} %get-tuple-element.6) | data formatting | bytes 4194304 | tf_op jit(solution)/shard_map/reshape | solution.py:18
  144.7 2.1 reshape.55
  146.8 4.2 %fusion.47 = (f32[8,4,64]{2,1,0:T(4,128)S(1)}, f32[8,4,64,256]{3,2,1,0:T(8,128)}) fusion(f32[8,256]{1,0:T(8,128)S(1)} %convert_element_type.53, pred[8,256]{1,0:T(8,128)(4,1)S(1)} %gt.23, bf16[8,256,4,128]{3,2,1,0:T(4,128)(2,1)} %reshape.55, bf16[8,64,4,128]{3,2,1,0:T(4,128)(2,1)S(1)} %reshape.49), kind=kOutput, calls=%fused_computation.56 | convolution fusion | flops 136839424 | bytes 4737024 | tf_op jit(solution)/shard_map/sub | solution.py:31
  151.0 2.3 fusion.27
  153.3 0.4 copy.33
  153.7 0.1 copy-done
  153.8 5.6 %fusion.35 = f32[512,4096]{1,0:T(8,128)} fusion(bf16[512,4096]{1,0:T(8,128)(2,1)S(1)} %copy-done, bf16[64,8,4,128]{3,2,1,0:T(4,128)(2,1)S(1)} %bitcast.21), kind=kOutput, calls=%fused_computation.34 | convolution fusion | flops 2147483648 | bytes 13107200 | tf_op jit(solution)/shard_map/dot_general | solution.py:110
  159.4 0.0 reduce-scatter.2.cloned.1.call-update
  159.4 95.3 %reduce-scatter.2.cloned.1.call-done = f32[512,512]{1,0:T(8,128)} async-done(((f32[512,4096]{1,0:T(8,128)}), f32[512,512]{1,0:T(8,128)}) %reduce-scatter.2.cloned.1.call-update) | async-done | bytes 1048592 | tf_op jit(solution)/shard_map/reduce_scatter | solution.py:111
  254.7 2.2 add_convert_fusion
  (20 shorter events, 0.1 us)
Async XLA Ops:
  6.5 56.8 %copy-start.2 = (bf16[512,512]{1,0:T(8,128)(2,1)S(1)}, bf16[512,512]{1,0:T(8,128)(2,1)}, u32[]{:S(2)}) copy-start(bf16[512,512]{1,0:T(8,128)(2,1)} %param.9) | copy-start | bytes 1572868
  6.5 101.1 %all-gather.3.cloned.1.call-start = ((), (), s32[]{:S(2)}) async-start(), calls=%async_computation.1 | async-start | bytes 17825792 | tf_op jit(solution)/shard_map/all_gather | solution.py:91
  7.3 247.5 %reduce-scatter.2.cloned.1.call-start = ((), (), s32[]{:S(2)}) async-start(), calls=%async_computation.2 | async-start | bytes 9437184 | tf_op jit(solution)/shard_map/reduce_scatter | solution.py:111
  7.3 18.3 %collective-permute-start = (bf16[512,512]{1,0:T(8,128)(2,1)}, bf16[512,512]{1,0:T(8,128)(2,1)S(1)}, u32[]{:S(2)}, u32[]{:S(2)}) collective-permute-start(bf16[512,512]{1,0:T(8,128)(2,1)} %param.9), channel_id=1, source_target_pairs={{0,1},{1,2},{2,3},{3,4},{4,5},{5,6},{6,7},{7,0},{8,9},{9,10},{10,1... | collective-permute-start | bytes 1572872 | tf_op jit(solution)/shard_map/ppermute | solution.py:61
  9.8 15.8 %collective-permute-start.1 = (bf16[512,512]{1,0:T(8,128)(2,1)}, bf16[512,512]{1,0:T(8,128)(2,1)S(1)}, u32[]{:S(2)}, u32[]{:S(2)}) collective-permute-start(bf16[512,512]{1,0:T(8,128)(2,1)} %param.9), channel_id=1, source_target_pairs={{0,7},{1,0},{2,1},{3,2},{4,3},{5,4},{6,5},{7,6},{8,15},{9,8},{10,9... | collective-permute-start | bytes 1572872 | tf_op jit(solution)/shard_map/ppermute | solution.py:71
  25.6 13.4 %collective-permute-start.2 = (bf16[512,512]{1,0:T(8,128)(2,1)S(1)}, bf16[512,512]{1,0:T(8,128)(2,1)S(1)}, u32[]{:S(2)}, u32[]{:S(2)}) collective-permute-start(bf16[512,512]{1,0:T(8,128)(2,1)S(1)} %collective-permute-done), channel_id=1, source_target_pairs={{0,1},{1,2},{2,3},{3,4},{4,5},{5,6},{6,7},{7,0},{8,9},{9,10},{10,1... | collective-permute-start | bytes 1572872 | tf_op jit(solution)/shard_map/ppermute | solution.py:61
  25.6 37.8 %collective-permute-start.3 = (bf16[512,512]{1,0:T(8,128)(2,1)S(1)}, bf16[512,512]{1,0:T(8,128)(2,1)S(1)}, u32[]{:S(2)}, u32[]{:S(2)}) collective-permute-start(bf16[512,512]{1,0:T(8,128)(2,1)S(1)} %collective-permute-done.1), channel_id=1, source_target_pairs={{0,7},{1,0},{2,1},{3,2},{4,3},{5,4},{6,5},{7,6},{8,15},{9,8},{10,9... | collective-permute-start | bytes 1572872 | tf_op jit(solution)/shard_map/ppermute | solution.py:71
  39.1 27.5 %collective-permute-start.4 = (bf16[512,512]{1,0:T(8,128)(2,1)S(1)}, bf16[512,512]{1,0:T(8,128)(2,1)S(1)}, u32[]{:S(2)}, u32[]{:S(2)}) collective-permute-start(bf16[512,512]{1,0:T(8,128)(2,1)S(1)} %collective-permute-done.2), channel_id=1, source_target_pairs={{0,1},{1,2},{2,3},{3,4},{4,5},{5,6},{6,7},{7,0},{8,9},{9,10},{10,1... | collective-permute-start | bytes 1572872 | tf_op jit(solution)/shard_map/ppermute | solution.py:61
  63.4 14.1 %collective-permute-start.5 = (bf16[512,512]{1,0:T(8,128)(2,1)S(1)}, bf16[512,512]{1,0:T(8,128)(2,1)S(1)}, u32[]{:S(2)}, u32[]{:S(2)}) collective-permute-start(bf16[512,512]{1,0:T(8,128)(2,1)S(1)} %collective-permute-done.3), channel_id=1, source_target_pairs={{0,7},{1,0},{2,1},{3,2},{4,3},{5,4},{6,5},{7,6},{8,15},{9,8},{10,9... | collective-permute-start | bytes 1572872 | tf_op jit(solution)/shard_map/ppermute | solution.py:71
  66.5 14.8 %collective-permute-start.6 = (bf16[512,512]{1,0:T(8,128)(2,1)S(1)}, bf16[512,512]{1,0:T(8,128)(2,1)S(1)}, u32[]{:S(2)}, u32[]{:S(2)}) collective-permute-start(bf16[512,512]{1,0:T(8,128)(2,1)S(1)} %collective-permute-done.4), channel_id=1, source_target_pairs={{0,1},{1,2},{2,3},{3,4},{4,5},{5,6},{6,7},{7,0},{8,9},{9,10},{10,1... | collective-permute-start | bytes 1572872 | tf_op jit(solution)/shard_map/ppermute | solution.py:61
  67.2 15.1 %copy-start.3 = (bf16[4096,512]{1,0:T(8,128)(2,1)S(1)}, bf16[4096,512]{1,0:T(8,128)(2,1)}, u32[]{:S(2)}) copy-start(bf16[4096,512]{1,0:T(8,128)(2,1)} %param.14) | copy-start | bytes 12582916
  67.2 15.0 %copy-start.6 = (f32[4096]{0:T(1024)S(1)}, f32[4096]{0:T(1024)}, u32[]{:S(2)}) copy-start(f32[4096]{0:T(1024)} %param.10) | copy-start | bytes 49156
  131.4 2.6 copy-start.4
  131.4 2.6 copy-start.5
  146.8 4.2 %copy-start.1 = (bf16[8,256,4,128]{3,2,1,0:T(4,128)(2,1)S(1)}, bf16[8,256,4,128]{3,2,1,0:T(4,128)(2,1)}, u32[]{:S(2)}) copy-start(bf16[8,256,4,128]{3,2,1,0:T(4,128)(2,1)} %reshape.56) | copy-start | bytes 6291460
  151.0 2.8 %copy-start = (bf16[512,4096]{1,0:T(8,128)(2,1)S(1)}, bf16[512,4096]{1,0:T(8,128)(2,1)}, u32[]{:S(2)}) copy-start(bf16[512,4096]{1,0:T(8,128)(2,1)} %param.17) | copy-start | bytes 12582916
Sparse Core Ops, SparseCore 0:
  9.2 98.4 all-gather.2
  159.5 95.1 reduce-scatter.1
